TPU v7x, 32 devices: a whole 2x2x4 slice. The times are simulated.
32 devices in a mesh: clips: 2 (over y), tm: 4 (over x, core), rows: 4 (over z).
Axes of the slice: x: 2, y: 2, z: 4, core: 2. Of those that a mesh axis runs over, the one named last changes fastest.
Arguments:
- segment_input: bfloat16 [4, 8, 4, 32, 384], P('clips', 'tm', 'rows'), parts along dimension 0, may hold values from -6 to 6
- inner_input: bfloat16 [4, 8, 4, 32, 384], P('clips', 'tm', 'rows'), parts along dimension 0, may hold values from -6 to 6
- lengths: int32 [4, 4], P('clips', 'tm'), parts along dimension 0, may hold values from 1 to 2
- inner_gain: float32 [384], replicated, may hold values from 0.25 to 1.75
- causal_weight: bfloat16 [3, 3, 3, 384, 384], replicated, may hold values from -0.0625 to 0.0625
- causal_bias: float32 [384], replicated, may hold values from -3 to 3
- attention_gain: float32 [384], replicated, may hold values from 0.25 to 1.75
- triple_weight: bfloat16 [384, 1152], replicated, may hold values from -0.4375 to 0.4375
- triple_bias: float32 [1152], replicated, may hold values from -150 to 150
- output_weight: bfloat16 [384, 384], replicated, may hold values from -0.3125 to 0.3125
- output_bias: float32 [384], replicated, may hold values from -3 to 3
Outputs:
- encoded: bfloat16 [4, 8, 4, 32, 384], P('clips', 'tm', 'rows'), parts along dimension 0
There are 2 independent parts, one for each index of `clips`. A program takes and returns all parts, laid end to end along the dimension named above; an argument that names none is the same for every part. Nothing has to cross between parts.
Inputs may be any that keep to these rules, and one draw needn't show every extreme that they name: The valid frames of a clip in a section are that section's first lengths[b, s] frame slots.
All inputs are finite; a program needn't handle non-finite values.
Results may differ from a plain program's by a relative error of at most 0.0062.
Values may be sent and summed in bfloat16 or wider, within the bound.
No kernel may reach another device: no remote copies, remote signals or barrier semaphores. Data moves between devices by JAX's collectives and lax.ppermute only.
A program may use at most 128 MiB of HBM per device.

v0:
```python
import math
import jax
import jax.numpy as jnp
from jax import lax
from jax.sharding import PartitionSpec as P

EPSILON = 1e-06


def prefix(part, axis, combine, identity):
    place = lax.axis_index(axis)
    gathered = jax.tree.map(lambda a: lax.all_gather(a, axis), part)
    state = jax.tree.map(lambda a, e: jnp.zeros_like(a) + jnp.asarray(e, a.dtype), part, identity)

    def one(step, state):
        return combine(
            state, jax.tree.map(lambda a: lax.dynamic_index_in_dim(a, step, 0, False), gathered)
        )

    return lax.fori_loop(0, place, one, state)


def as_sent(x):

    def short(part):
        return part.astype(jnp.bfloat16) if part.dtype == jnp.float32 else part

    return jax.tree.map(short, x)


def with_halo(cells, sides, width):
    for axis, dim in sides:
        count = lax.axis_size(axis)
        ends = count - 1
        head = lax.slice_in_dim(cells, 0, width, axis=dim)
        tail = lax.slice_in_dim(cells, cells.shape[dim] - width, cells.shape[dim], axis=dim)
        cells = jnp.concatenate(
            [
                lax.ppermute(tail, axis, [(i, (i + 1) % count) for i in range(ends)]),
                cells,
                lax.ppermute(head, axis, [((i + 1) % count, i) for i in range(ends)]),
            ],
            axis=dim,
        )
    return cells


def normalize(field, gain):
    widened = field.astype(jnp.float32)
    return widened * lax.rsqrt(jnp.mean(widened * widened, axis=-1, keepdims=True) + EPSILON) * gain


def last_two(extended, counts):
    slot_total = extended.shape[1]
    chosen = []
    for position in range(2):
        target = counts + position
        picked = jnp.zeros_like(extended[:, 0])
        for slot_index in range(slot_total):
            matches = (target == slot_index)[:, None, None, None]
            picked = jnp.where(matches, extended[:, slot_index], picked)
        chosen.append(picked)
    return jnp.stack(chosen, axis=1)


def summarize(activated, counts):
    blanks = jnp.zeros((activated.shape[0], 2) + activated.shape[2:], activated.dtype)
    summary = last_two(jnp.concatenate([blanks, activated], axis=1), counts)
    return (summary, jnp.minimum(counts, 2).astype(jnp.bfloat16))


def join_later(earlier, later):
    early_frames, early_count = earlier
    late_frames, late_count = later
    complete = (late_count > 1.5)[:, None, None, None, None]
    single = (late_count > 0.5)[:, None, None, None, None]
    shifted = jnp.concatenate([early_frames[:, 1:], late_frames[:, 1:]], axis=1)
    frames = jnp.where(complete, late_frames, jnp.where(single, shifted, early_frames))
    total_count = jnp.minimum(early_count + late_count, 2.0).astype(early_count.dtype)
    return (frames, total_count)


def incoming_cache(summary, counts):
    starting = (jnp.zeros_like(summary), jnp.zeros_like(counts))
    combined = prefix((summary, counts), "tm", join_later, starting)
    return combined[0]


def convolve(padded, causal_weight, causal_bias):
    clip_count, slot_total, rows_padded, column_count, channels = padded.shape
    frame_count = slot_total - 2
    row_count = rows_padded - 2
    widened = jnp.pad(padded, ((0, 0), (0, 0), (0, 0), (1, 1), (0, 0)))
    summed = jnp.zeros((clip_count * frame_count * row_count * column_count, channels), jnp.float32)
    for delta_time in range(3):
        for delta_row in range(3):
            window = widened[
                :, delta_time : delta_time + frame_count, delta_row : delta_row + row_count
            ]
            columns = jnp.concatenate(
                [window[:, :, :, delta_col : delta_col + column_count] for delta_col in range(3)],
                axis=-1,
            )
            kernel = causal_weight[delta_time, delta_row].reshape(3 * channels, channels)
            summed = summed + jnp.dot(
                columns.reshape(-1, 3 * channels), kernel, preferred_element_type=jnp.float32
            )
    return summed.reshape(clip_count, frame_count, row_count, column_count, channels) + causal_bias


def attend(normed, triple_weight, triple_bias, output_weight, output_bias):
    frame_count, places, channels = normed.shape
    packed = (
        jnp.dot(normed.reshape(-1, channels), triple_weight, preferred_element_type=jnp.float32)
        + triple_bias
    )
    packed = packed.reshape(frame_count, places, 3 * channels)
    queries = packed[:, :, :channels]
    key_vectors = packed[:, :, channels : 2 * channels]
    values = packed[:, :, 2 * channels :].astype(jnp.bfloat16)
    scores = jnp.einsum(
        "nqc,nkc->nqk", queries, key_vectors, precision=lax.Precision.HIGHEST
    ) / math.sqrt(channels)
    row_max = jnp.max(scores, axis=-1, keepdims=True)
    exponent = jnp.exp(scores - row_max)
    weights = (exponent / jnp.sum(exponent, axis=-1, keepdims=True)).astype(jnp.bfloat16)
    attended = jnp.einsum(
        "nqk,nkc->nqc", weights, values, preferred_element_type=jnp.float32
    ).astype(jnp.bfloat16)
    projected = (
        jnp.dot(attended.reshape(-1, channels), output_weight, preferred_element_type=jnp.float32)
        + output_bias
    )
    return projected.reshape(frame_count, places, channels).astype(jnp.bfloat16)


def body(
    segment_input,
    inner_input,
    lengths,
    inner_gain,
    causal_weight,
    causal_bias,
    attention_gain,
    triple_weight,
    triple_bias,
    output_weight,
    output_bias,
):
    clip_count, frame_count, row_count, column_count, channels = segment_input.shape
    activated = jax.nn.silu(normalize(inner_input, inner_gain)).astype(jnp.bfloat16)
    counts = lengths[:, 0]
    live_mask = (jnp.arange(frame_count, dtype=jnp.int32)[None, :] < counts[:, None]).astype(
        jnp.float32
    )
    carried = incoming_cache(*summarize(activated, counts))
    extended = jnp.concatenate([carried, activated], axis=1)
    padded = with_halo(as_sent(extended), (("rows", 2),), 1).astype(extended.dtype)
    convolved = convolve(padded, causal_weight, causal_bias)
    residual = (segment_input.astype(jnp.float32) + convolved).astype(jnp.bfloat16)
    residual = lax.optimization_barrier(residual)
    normed = normalize(residual, attention_gain).astype(jnp.bfloat16)
    row_devices = lax.axis_size("rows")
    per_device = clip_count * frame_count // row_devices
    grouped = normed.reshape(row_devices, per_device, row_count, column_count, channels)
    portion = lax.all_to_all(grouped, "rows", split_axis=0, concat_axis=2, tiled=True)
    owned = portion.shape[1]
    height = portion.shape[2]
    flat = portion.reshape(owned, height * column_count, channels)
    result = attend(flat, triple_weight, triple_bias, output_weight, output_bias)
    result = result.reshape(1, owned, height, column_count, channels)
    projected = lax.all_to_all(result, "rows", split_axis=2, concat_axis=0, tiled=True)
    projected = projected.reshape(clip_count, frame_count, row_count, column_count, channels)
    projected = lax.optimization_barrier(projected)
    summed = residual.astype(jnp.float32) + projected.astype(jnp.float32)
    return (summed * live_mask[:, :, None, None, None]).astype(jnp.bfloat16)


def activate(field, gain):
    return jax.nn.silu(normalize(field, gain)).astype(jnp.bfloat16)


def conv3d(frames, causal_weight, time_padding):
    return lax.conv_general_dilated(
        frames,
        causal_weight,
        window_strides=(1, 1, 1),
        padding=(time_padding, (1, 1), (1, 1)),
        dimension_numbers=("NDHWC", "DHWIO", "NDHWC"),
        preferred_element_type=jnp.float32,
    )


def gathered_body(
    segment_input,
    inner_input,
    lengths,
    inner_gain,
    causal_weight,
    causal_bias,
    attention_gain,
    triple_weight,
    triple_bias,
    output_weight,
    output_bias,
):
    clip_count, frame_count, row_count, column_count, channels = segment_input.shape
    sections = lax.axis_size("tm")
    counts = lengths[:, 0]
    ahead = [(i, i + 1) for i in range(sections - 1)]
    prev_counts = lax.ppermute(counts, "tm", ahead)
    both = jnp.concatenate([inner_input, segment_input], axis=0)
    both_all = lax.all_gather(both, "rows", axis=2, tiled=True)
    inner_all = both_all[:clip_count]
    segment_all = both_all[clip_count:]
    wide = (counts > 1)[:, None, None, None]
    last_raw = jnp.where(wide, inner_all[:, frame_count - 1], inner_all[:, 0])
    prev_raw = lax.ppermute(inner_all, "tm", ahead)
    before_raw = lax.ppermute(last_raw, "tm", [(i, i + 2) for i in range(sections - 2)])
    own = activate(inner_all, inner_gain)
    own_part = conv3d(own, causal_weight, (2, 0))
    prev = activate(prev_raw, inner_gain)
    before = activate(before_raw, inner_gain)
    prev_wide = (prev_counts > 1)[:, None, None, None]
    carried = jnp.stack(
        [
            jnp.where(prev_wide, prev[:, frame_count - 2], before),
            jnp.where(prev_wide, prev[:, frame_count - 1], prev[:, 0]),
        ],
        axis=1,
    )
    carried_part = conv3d(carried, causal_weight, (0, frame_count))
    convolved = own_part + carried_part + causal_bias
    residual = (segment_all.astype(jnp.float32) + convolved).astype(jnp.bfloat16)
    normed = normalize(residual, attention_gain).astype(jnp.bfloat16)
    height = normed.shape[2]
    frames = clip_count * frame_count
    places = height * column_count
    flat = normed.reshape(frames * places, channels)
    packed = (
        jnp.dot(flat, triple_weight[:, channels:], preferred_element_type=jnp.float32)
        + triple_bias[channels:]
    ).reshape(frames, places, 2 * channels)
    key_vectors = packed[:, :, :channels]
    values = packed[:, :, channels:].astype(jnp.bfloat16)
    start = lax.axis_index("rows") * row_count
    mine = lax.dynamic_slice_in_dim(normed, start, row_count, axis=2)
    queries = (
        jnp.dot(
            mine.reshape(-1, channels),
            triple_weight[:, :channels],
            preferred_element_type=jnp.float32,
        )
        + triple_bias[:channels]
    ).reshape(frames, row_count * column_count, channels)
    scores = jnp.einsum(
        "nqc,nkc->nqk", queries, key_vectors, precision=lax.Precision.HIGHEST
    ) / math.sqrt(channels)
    row_max = jnp.max(scores, axis=-1, keepdims=True)
    exponent = jnp.exp(scores - row_max)
    weights = (exponent / jnp.sum(exponent, axis=-1, keepdims=True)).astype(jnp.bfloat16)
    attended = jnp.einsum(
        "nqk,nkc->nqc", weights, values, preferred_element_type=jnp.float32
    ).astype(jnp.bfloat16)
    projected = (
        jnp.dot(attended.reshape(-1, channels), output_weight, preferred_element_type=jnp.float32)
        + output_bias
    ).astype(jnp.bfloat16)
    projected = projected.reshape(clip_count, frame_count, row_count, column_count, channels)
    residual_mine = lax.dynamic_slice_in_dim(residual, start, row_count, axis=2)
    live_mask = (jnp.arange(frame_count, dtype=jnp.int32)[None, :] < counts[:, None]).astype(
        jnp.float32
    )
    summed = residual_mine.astype(jnp.float32) + projected.astype(jnp.float32)
    return (summed * live_mask[:, :, None, None, None]).astype(jnp.bfloat16)


GATHER_LIMIT = 1 << 22


def chosen_body(segment_input, inner_input, *rest):
    gathered = inner_input.size * inner_input.dtype.itemsize * lax.axis_size("rows")
    if gathered <= GATHER_LIMIT:
        return gathered_body(segment_input, inner_input, *rest)
    return body(segment_input, inner_input, *rest)


def solution(mesh):
    placed = (
        P("clips", "tm", "rows", None, None),
        P("clips", "tm", "rows", None, None),
        P("clips", "tm"),
        P(),
        P(),
        P(),
        P(),
        P(),
        P(),
        P(),
        P(),
    )
    return jax.shard_map(
        chosen_body,
        mesh=mesh,
        in_specs=placed,
        out_specs=P("clips", "tm", "rows", None, None),
        check_vma=False,
    )
```

profile of v0, /device:TPU:1, one launch (start us, length us, event | category | flops | bytes accessed | tf_op | source)
XLA Modules:
  0.0 64.8 jit_solution(6598093223761162605)
XLA Ops:
  0.0 4.6 %collective-permute-start = (s32[2]{0:T(128)}, s32[2]{0:T(128)S(1)}, u32[]{:S(2)}, u32[]{:S(2)}) collective-permute-start(s32[2]{0:T(128)} %bitcast.72), channel_id=1, source_target_pairs={{0,4},{4,8},{8,12},{1,5},{5,9},{9,13},{2,6},{6,10},{10,14},{3,7},{... | collective-permute-start | bytes 32 | tf_op jit(solution)/shard_map/ppermute | solution.py:211
  4.6 0.7 %broadcast_compare_fusion = pred[2]{0:T(512)(128)(4,1)S(1)} fusion(s32[2,1]{0,1:T(1,128)} %param.13), kind=kLoop, calls=%fused_computation.89 | loop fusion | flops 2 | bytes 10 | tf_op jit(solution)/shard_map/gt | solution.py:216
  5.3 1.0 %pad_maximum_fusion = bf16[4,2,1,32,384]{4,3,1,0,2:T(8,128)(2,1)S(1)} fusion(bf16[2,2,1,32,384]{4,3,1,0,2:T(8,128)(2,1)} %bitcast.70, bf16[2,2,1,32,384]{4,3,1,0,2:T(8,128)(2,1)} %bitcast.71), kind=kLoop, calls=%fused_computation.71 | loop fusion | flops 98304 | bytes 393216 | tf_op jit(solution)/shard_map/concatenate | solution.py:212
  6.3 17.9 %all_gather.3 = bf16[4,2,4,32,384]{4,3,1,0,2:T(8,128)(2,1)S(1)} all-gather(bf16[4,2,1,32,384]{4,3,1,0,2:T(8,128)(2,1)S(1)} %pad_maximum_fusion), channel_id=1, replica_groups=mesh['clips'=2,'tm'=4,'rows'=4] {'rows'}, dimensions={2}, use_global_device_ids=true | all-gather | bytes 983040 | tf_op jit(solution)/shard_map/all_gather | solution.py:213
  24.3 1.3 %collective-permute-start.2 = (bf16[2,4,32,384]{3,2,0,1:T(8,128)(2,1)S(1)}, bf16[2,4,32,384]{3,2,0,1:T(8,128)(2,1)S(1)}, u32[]{:S(2)}, u32[]{:S(2)}) collective-permute-start(bf16[2,4,32,384]{3,2,0,1:T(8,128)(2,1)S(1)} %fusion.48), channel_id=1, source_target_pairs={{0,8},{4,12},{1,9},{5,13},{2,10},{6,14},{3,11},{7,15},{16,24},{20,... | collective-permute-start | bytes 589832 | tf_op jit(solution)/shard_map/ppermute | solution.py:219
  25.8 3.9 %collective-permute-start.1 = (bf16[2,2,4,32,384]{4,3,0,2,1:T(8,128)(2,1)S(1)}, bf16[2,2,4,32,384]{4,3,0,2,1:T(8,128)(2,1)S(1)}, u32[]{:S(2)}, u32[]{:S(2)}) collective-permute-start(bf16[2,2,4,32,384]{4,3,0,2,1:T(8,128)(2,1)S(1)} %copy.107), channel_id=1, source_target_pairs={{0,4},{4,8},{8,12},{1,5},{5,9},{9,13},{2,6},{6,10},{10,14},{3,7},{... | collective-permute-start | bytes 1179656 | tf_op jit(solution)/shard_map/ppermute | solution.py:218
  29.8 0.2 fusion.8
  30.1 5.5 %collective-permute-done.1 = bf16[2,2,4,32,384]{4,3,0,2,1:T(8,128)(2,1)S(1)} collective-permute-done((bf16[2,2,4,32,384]{4,3,0,2,1:T(8,128)(2,1)S(1)}, bf16[2,2,4,32,384]{4,3,0,2,1:T(8,128)(2,1)S(1)}, u32[]{:S(2)}, u32[]{:S(2)}) %collective-permute-start.1) | collective-permute-done | bytes 393248 | tf_op jit(solution)/shard_map/ppermute | solution.py:218
  35.6 0.2 fusion.16
  35.8 0.5 fusion.45
  36.3 0.3 copy.110
  36.7 0.4 pad.clone
  37.0 0.1 slice.57
  37.1 0.6 fusion.30
  37.8 0.2 fusion.51
  38.1 0.3 copy.111
  38.5 0.4 pad.2.clone
  39.0 0.6 fusion.31
  39.6 13.2 %convolution_select_fusion = f32[2,4,16,5,384]{4,2,3,1,0:T(8,128)S(1)} fusion(bf16[3,3,3,384,384]{4,3,2,1,0:T(8,128)(2,1)} %param.15, bf16[2,4,2,8,7,384]{5,2,4,3,1,0:T(2,128)(2,1)S(1)} %fusion.31, pred[16,5]{0,1:T(8,128)(4,1)S(1)} %copy-done.4), kind=kOutput, calls=%fused_computation.5 | convolution fusion | flops 2123612160 | bytes 9633872 | tf_op jit(solution)/shard_map/conv_general_dilated | solution.py:184
  52.8 7.0 %fusion.4 = f32[2,4,16,5,384]{4,2,3,1,0:T(8,128)S(1)} fusion(f32[2,4,16,5,384]{4,2,3,1,0:T(8,128)S(1)} %convolution_select_fusion, bf16[3,3,3,384,384]{4,3,2,1,0:T(8,128)(2,1)S(1)} %bitcast.57, bf16[2,4,2,8,7,384]{5,2,4,3,1,0:T(2,128)(2,1)S(1)} %fusion.30, f32[384]{0:T(512)S(1)} %copy-done.5, pred[16,5]{0,1:T(8,128)(4,1)S(1)} %copy-done.4), kind=kOutput, calls=%fused_computation.8 | convolution fusion | flops 2124103680 | bytes 10618448 | tf_op jit(solution)/shard_map/conv_general_dilated | solution.py:184
  59.9 0.4 copy.101
  60.4 0.2 fusion.24
  60.6 0.3 copy-done.6
  60.9 0.2 fusion.26
  61.1 0.4 copy-done.1
  61.5 0.2 convolution_add_fusion.2
  61.7 0.6 convolution_add_fusion
  62.3 0.9 %convolution_multiply_fusion = f32[4,32,128]{2,1,0:T(8,128)S(1)} fusion(f32[4,32,384]{2,1,0:T(8,128)S(1)} %bitcast.66, f32[4,128,768]{2,1,0:T(8,128)S(1)} %bitcast.58), kind=kOutput, calls=%fused_computation.15 | convolution fusion | flops 75513856 | bytes 1048576 | tf_op jit(solution)/shard_map/nqc,nkc->nqk/dot_general | solution.py:256
  63.3 0.2 fusion.60
  63.5 0.3 convolution_convert_fusion
  63.8 0.2 fusion.5
  64.0 0.7 %fusion.50 = bf16[2,2,1,32,384]{4,3,2,1,0:T(8,128)(2,1)} fusion(bf16[2,2,1,32,384]{4,3,2,1,0:T(8,128)(2,1)S(1)} %bitcast.69, f32[2,2]{1,0:T(2,128)S(1)} %compare_convert_fusion, bf16[2,2,4,32,384]{4,3,2,1,0:T(8,128)(2,1)S(1)} %get-tuple-element.6, s32[]{:T(128)S(6)} %select_n.18), kind=kLoop, calls=%fused_computation.74 | loop fusion | flops 245760 | bytes 294932 | tf_op jit(solution)/shard_map/convert_element_type | solution.py:275
  (43 shorter events, 1.0 us)
Async XLA Ops:
  0.0 63.8 %copy-start = (bf16[384,384]{1,0:T(8,128)(2,1)S(1)}, bf16[384,384]{1,0:T(8,128)(2,1)}, u32[]{:S(2)}) copy-start(bf16[384,384]{1,0:T(8,128)(2,1)} %param.20) | copy-start | bytes 884740
  0.0 30.0 %collective-permute-start = (s32[2]{0:T(128)}, s32[2]{0:T(128)S(1)}, u32[]{:S(2)}, u32[]{:S(2)}) collective-permute-start(s32[2]{0:T(128)} %bitcast.72), channel_id=1, source_target_pairs={{0,4},{4,8},{8,12},{1,5},{5,9},{9,13},{2,6},{6,10},{10,14},{3,7},{... | collective-permute-start | bytes 32 | tf_op jit(solution)/shard_map/ppermute | solution.py:211
  24.2 5.5 %copy-start.8 = (s32[2,1]{0,1:T(1,128)S(1)}, s32[2,1]{0,1:T(1,128)}, u32[]{:S(2)}) copy-start(s32[2,1]{0,1:T(1,128)} %param.13) | copy-start | bytes 28
  24.2 5.6 %copy-start.3 = (f32[1152]{0:T(1024)S(1)}, f32[1152]{0:T(1024)}, u32[]{:S(2)}) copy-start(f32[1152]{0:T(1024)} %param.19) | copy-start | bytes 13828
  24.3 11.5 %copy-start.2 = (f32[384]{0:T(512)S(1)}, f32[384]{0:T(512)}, u32[]{:S(2)}) copy-start(f32[384]{0:T(512)} %param.14) | copy-start | bytes 4612
  24.3 5.7 %collective-permute-start.2 = (bf16[2,4,32,384]{3,2,0,1:T(8,128)(2,1)S(1)}, bf16[2,4,32,384]{3,2,0,1:T(8,128)(2,1)S(1)}, u32[]{:S(2)}, u32[]{:S(2)}) collective-permute-start(bf16[2,4,32,384]{3,2,0,1:T(8,128)(2,1)S(1)} %fusion.48), channel_id=1, source_target_pairs={{0,8},{4,12},{1,9},{5,13},{2,10},{6,14},{3,11},{7,15},{16,24},{20,... | collective-permute-start | bytes 589832 | tf_op jit(solution)/shard_map/ppermute | solution.py:219
  25.8 9.8 %collective-permute-start.1 = (bf16[2,2,4,32,384]{4,3,0,2,1:T(8,128)(2,1)S(1)}, bf16[2,2,4,32,384]{4,3,0,2,1:T(8,128)(2,1)S(1)}, u32[]{:S(2)}, u32[]{:S(2)}) collective-permute-start(bf16[2,2,4,32,384]{4,3,0,2,1:T(8,128)(2,1)S(1)} %copy.107), channel_id=1, source_target_pairs={{0,4},{4,8},{8,12},{1,5},{5,9},{9,13},{2,6},{6,10},{10,14},{3,7},{... | collective-permute-start | bytes 1179656 | tf_op jit(solution)/shard_map/ppermute | solution.py:218
  38.1 1.4 %copy-start.4 = (pred[16,5]{0,1:T(8,128)(4,1)S(1)}, pred[16,5]{0,1:T(8,128)(4,1)}, u32[]{:S(2)}) copy-start(pred[16,5]{0,1:T(8,128)(4,1)} %constant.44) | copy-start | bytes 244
  39.0 13.8 %slice-start = ((s8[7962624]{0:T(1024)(128)(4,1)}), s8[4194304]{0:T(1024)(128)(4,1)S(1)}, s32[]{:S(2)}) async-start(s8[7962624]{0:T(1024)(128)(4,1)} %bitcast.56), calls=%async_computation | async-start | bytes 8388608
  39.6 13.2 %slice-start.1 = ((s8[7962624]{0:T(1024)(128)(4,1)}), s8[3768320]{0:T(1024)(128)(4,1)S(1)}, s32[]{:S(2)}) async-start(s8[7962624]{0:T(1024)(128)(4,1)} %bitcast.56), calls=%async_computation.1 | async-start | bytes 7536640
  39.6 13.2 %copy-start.5 = (f32[384]{0:T(512)S(1)}, f32[384]{0:T(512)}, u32[]{:S(2)}) copy-start(f32[384]{0:T(512)} %param.16) | copy-start | bytes 4612
  60.2 0.7 %copy-start.6 = (f32[384]{0:T(512)S(1)}, f32[384]{0:T(512)}, u32[]{:S(2)}) copy-start(f32[384]{0:T(512)} %param.17) | copy-start | bytes 4612
  60.3 1.2 %copy-start.1 = (bf16[384,1152]{1,0:T(8,128)(2,1)S(1)}, bf16[384,1152]{1,0:T(8,128)(2,1)}, u32[]{:S(2)}) copy-start(bf16[384,1152]{1,0:T(8,128)(2,1)} %param.18) | copy-start | bytes 2654212
  60.4 1.2 %slice-start.2 = ((f32[1152]{0:T(1024)}), f32[384]{0:T(512)S(1)}, s32[]{:S(2)}) async-start(f32[1152]{0:T(1024)} %param.19), calls=%async_computation.2 | async-start | bytes 4096 | tf_op jit(solution)/shard_map/slice | solution.py:254
  62.3 1.5 %copy-start.7 = (f32[384]{0:T(512)S(1)}, f32[384]{0:T(512)}, u32[]{:S(2)}) copy-start(f32[384]{0:T(512)} %param.21) | copy-start | bytes 4612
where the time goes:
time: 65 us; the launch traced here: 64.8 us
  matrix products  22.4 us (34%)
  blocking collectives  17.9 us (28%)
  starting transfers between devices  9.81 us (15%)
  other arithmetic  5.62 us (9%)
  waiting for transfers between devices  5.46 us (8%)
  local copies, waits for them, and re-layouts  3.06 us (5%)
    conv_general_dilated x2, matrix products, conv3d(): lax.conv_general_dilated(frames, causal_weight, window_strides=(1, 1, 1),...  20.2 us
    all_gather x1, blocking collectives, gathered_body(): both_all = lax.all_gather(both, 'rows', axis=2, tiled=True)  17.9 us
    ppermute x1, waiting for transfers between devices, gathered_body(): prev_raw = lax.ppermute(inner_all, 'tm', ahead)  5.46 us
    ppermute x1, starting transfers between devices, gathered_body(): prev_counts = lax.ppermute(counts, 'tm', ahead)  4.63 us
    ppermute x1, starting transfers between devices, gathered_body(): prev_raw = lax.ppermute(inner_all, 'tm', ahead)  3.88 us
    unnamed x25, local copies, waits for them, and re-layouts  1.5 us
    ppermute x1, starting transfers between devices, gathered_body(): lax.ppermute(last_raw, 'tm', [(i, i + 2) for i in range(sections - 2)])  1.3 us
  transfers between devices with their start and end apart: 3, of which 1 were waited for; matrix products, arithmetic and copies ran while one was open for 3% of the time, Pallas kernels for 0%

commit v1 on v0

--- a/solution.py
+++ b/solution.py
@@ -5,6 +5,19 @@
 from jax.sharding import PartitionSpec as P
 
 EPSILON = 1e-06
+
+
+def ring_gather(x, axis, dim):
+    ways = lax.axis_size(axis)
+    up = [(d, (d + 1) % ways) for d in range(ways)]
+    down = [(d, (d - 1) % ways) for d in range(ways)]
+    earlier, later = ([x], [x])
+    for _ in range(ways // 2):
+        earlier.append(lax.ppermute(earlier[-1], axis, up))
+    for _ in range((ways - 1) // 2):
+        later.append(lax.ppermute(later[-1], axis, down))
+    line = jnp.concatenate([*earlier[::-1], *later[1:]], axis=dim)
+    return jnp.roll(line, (lax.axis_index(axis) - ways // 2) * x.shape[dim], axis=dim)
 
 
 def prefix(part, axis, combine, identity):
@@ -210,7 +223,7 @@
     ahead = [(i, i + 1) for i in range(sections - 1)]
     prev_counts = lax.ppermute(counts, "tm", ahead)
     both = jnp.concatenate([inner_input, segment_input], axis=0)
-    both_all = lax.all_gather(both, "rows", axis=2, tiled=True)
+    both_all = ring_gather(both, "rows", 2)
     inner_all = both_all[:clip_count]
     segment_all = both_all[clip_count:]
     wide = (counts > 1)[:, None, None, None]

time: 65 us -> 59 us (0.908)
  blocking collectives: 17.9 us -> 0 us
  waiting for transfers between devices: 5.46 us -> 13.8 us
  matrix products: 22.4 us -> 16.5 us
  starting transfers between devices: 9.81 us -> 14.8 us
  local copies, waits for them, and re-layouts: 3.06 us -> 7.76 us
    all_gather x1 -> x0, blocking collectives: 17.9 us -> none  [gathered_body(): both_all = lax.all_gather(both, 'rows', axis=2, tiled=True)]
    ppermute x1, waiting for transfers between devices: 0.01 us -> 7.49 us  [gathered_body(): lax.ppermute(last_raw, 'tm', [(i, i + 2) for i in range(sections - 2)])]
    ppermute x0 -> x3, waiting for transfers between devices: none -> 6.3 us  [the longest x2 6.29 us: ring_gather(): earlier.append(lax.ppermute(earlier[-1], axis, up))]
    conv_general_dilated x2, matrix products: 20.2 us -> 14.2 us  [conv3d(): lax.conv_general_dilated(frames, causal_weight, window_strides=(1, 1, 1),...]
    ppermute x1, waiting for transfers between devices: 5.46 us -> 0.01 us  [gathered_body(): prev_raw = lax.ppermute(inner_all, 'tm', ahead)]
    ppermute x0 -> x3, starting transfers between devices: none -> 4.27 us  [the longest x2 2.18 us: ring_gather(): earlier.append(lax.ppermute(earlier[-1], axis, up))]
    unnamed x25 -> x35, local copies, waits for them, and re-layouts: 1.5 us -> 4.63 us
    ppermute x1, starting transfers between devices: 3.88 us -> 5.15 us  [gathered_body(): prev_raw = lax.ppermute(inner_all, 'tm', ahead)]
  transfers between devices with their start and end apart: 3 -> 6, of which waited for: 1 -> 2; matrix products, arithmetic and copies ran while one was open for 3% -> 7% of each run, Pallas kernels for 0% -> 0%
where the time goes in v1:
time: 59 us; the launch traced here: 58.7 us
  matrix products  16.5 us (28%)
  starting transfers between devices  14.8 us (25%)
  waiting for transfers between devices  13.8 us (23%)
  local copies, waits for them, and re-layouts  7.76 us (13%)
  other arithmetic  5.32 us (9%)
    conv_general_dilated x2, matrix products, conv3d(): lax.conv_general_dilated(frames, causal_weight, window_strides=(1, 1, 1),...  14.2 us
    ppermute x1, waiting for transfers between devices, gathered_body(): lax.ppermute(last_raw, 'tm', [(i, i + 2) for i in range(sections - 2)])  7.49 us
    ppermute x2, waiting for transfers between devices, ring_gather(): earlier.append(lax.ppermute(earlier[-1], axis, up))  6.29 us
    ppermute x1, starting transfers between devices, gathered_body(): prev_raw = lax.ppermute(inner_all, 'tm', ahead)  5.15 us
    unnamed x35, local copies, waits for them, and re-layouts  4.63 us
    ppermute x1, starting transfers between devices, gathered_body(): prev_counts = lax.ppermute(counts, 'tm', ahead)  4.11 us
    ppermute x2, starting transfers between devices, ring_gather(): earlier.append(lax.ppermute(earlier[-1], axis, up))  2.18 us
    ppermute x1, starting transfers between devices, ring_gather(): later.append(lax.ppermute(later[-1], axis, down))  2.09 us
  transfers between devices with their start and end apart: 6, of which 2 were waited for; matrix products, arithmetic and copies ran while one was open for 7% of the time, Pallas kernels for 0%

profile of v1, /device:TPU:1, one launch (start us, length us, event | category | flops | bytes accessed | tf_op | source)
XLA Modules:
  0.0 58.7 jit_solution(10241180790332955674)
XLA Ops:
  0.0 1.0 %constant_dynamic-update-slice_fusion.1 = bf16[4,2,1,32,384]{4,3,2,1,0:T(8,128)(2,1)S(1)} fusion(bf16[2,2,1,32,384]{4,3,2,1,0:T(8,128)(2,1)} %param.12), kind=kLoop, calls=%fused_computation.78 | loop fusion | bytes 196608
  1.0 0.9 %constant_dynamic-update-slice_fusion = bf16[4,2,1,32,384]{4,3,2,1,0:T(8,128)(2,1)S(1)} fusion(bf16[4,2,1,32,384]{4,3,2,1,0:T(8,128)(2,1)S(1)} %constant_dynamic-update-slice_fusion.1, bf16[2,2,1,32,384]{4,3,2,1,0:T(8,128)(2,1)} %param.11), kind=kLoop, calls=%fused_computation.77 | loop fusion | bytes 196608 | tf_op jit(solution)/shard_map/concatenate | solution.py:225
  1.9 2.2 %collective-permute-start = (bf16[4,2,1,32,384]{4,3,2,1,0:T(8,128)(2,1)S(1)}, bf16[4,2,1,32,384]{4,3,2,1,0:T(8,128)(2,1)S(1)}, u32[]{:S(2)}, u32[]{:S(2)}) collective-permute-start(bf16[4,2,1,32,384]{4,3,2,1,0:T(8,128)(2,1)S(1)} %constant_dynamic-update-slice_fusion), channel_id=1, source_target_pairs={{0,1},{1,2},{2,3},{3,0},{4,5},{5,6},{6,7},{7,4},{8,9},{9,10},{10,1... | collective-permute-start | bytes 589832 | tf_op jit(solution)/shard_map/ppermute | solution.py:16
  4.1 2.1 %collective-permute-start.2 = (bf16[4,2,1,32,384]{4,3,2,1,0:T(8,128)(2,1)S(1)}, bf16[4,2,1,32,384]{4,3,2,1,0:T(8,128)(2,1)S(1)}, u32[]{:S(2)}, u32[]{:S(2)}) collective-permute-start(bf16[4,2,1,32,384]{4,3,2,1,0:T(8,128)(2,1)S(1)} %constant_dynamic-update-slice_fusion), channel_id=1, source_target_pairs={{0,3},{1,0},{2,1},{3,2},{4,7},{5,4},{6,5},{7,6},{8,11},{9,8},{10,9... | collective-permute-start | bytes 589832 | tf_op jit(solution)/shard_map/ppermute | solution.py:18
  6.2 4.1 %collective-permute-start.3 = (s32[2]{0:T(128)}, s32[2]{0:T(128)S(1)}, u32[]{:S(2)}, u32[]{:S(2)}) collective-permute-start(s32[2]{0:T(128)} %bitcast.68), channel_id=1, source_target_pairs={{0,4},{4,8},{8,12},{1,5},{5,9},{9,13},{2,6},{6,10},{10,14},{3,7},{... | collective-permute-start | bytes 32 | tf_op jit(solution)/shard_map/ppermute | solution.py:224
  10.3 0.7 %slice.49 = f32[768]{0:T(1024)S(1)} slice(f32[1152]{0:T(1024)} %param.19), slice={[384:1152]} | slice | bytes 6144 | tf_op jit(solution)/shard_map/slice | solution.py:255
  11.0 0.7 %compare_convert_fusion = f32[2,2]{1,0:T(2,128)S(1)} fusion(s32[2]{0:T(128)} %bitcast.69), kind=kLoop, calls=%fused_computation.95 | loop fusion | flops 8 | bytes 24 | tf_op jit(solution)/shard_map/convert_element_type | solution.py:284
  11.7 0.7 %broadcast_compare_fusion = pred[2]{0:T(512)(128)(4,1)S(1)} fusion(s32[2,1]{0,1:T(1,128)} %param.13), kind=kLoop, calls=%fused_computation.99 | loop fusion | flops 2 | bytes 10 | tf_op jit(solution)/shard_map/gt | solution.py:229
  12.4 6.3 %collective-permute-done.1 = bf16[4,2,1,32,384]{4,3,2,1,0:T(8,128)(2,1)S(1)} collective-permute-done((bf16[4,2,1,32,384]{4,3,2,1,0:T(8,128)(2,1)S(1)}, bf16[4,2,1,32,384]{4,3,2,1,0:T(8,128)(2,1)S(1)}, u32[]{:S(2)}, u32[]{:S(2)}) %collective-permute-start.1) | collective-permute-done | bytes 196640 | tf_op jit(solution)/shard_map/ppermute | solution.py:16
  18.8 0.9 %constant_dynamic-update-slice_fusion.9 = bf16[4,2,8,32,384]{4,3,2,1,0:T(8,128)(2,1)S(1)} fusion(bf16[4,2,8,32,384]{4,3,2,1,0:T(8,128)(2,1)S(1)} %constant_dynamic-update-slice_fusion.10, bf16[2,2,1,32,384]{4,3,2,1,0:T(8,128)(2,1)} %param.12), kind=kLoop, calls=%fused_computation.86 | loop fusion | bytes 196608
  19.7 0.9 %constant_dynamic-update-slice_fusion.8 = bf16[4,2,8,32,384]{4,3,2,1,0:T(8,128)(2,1)S(1)} fusion(bf16[4,2,8,32,384]{4,3,2,1,0:T(8,128)(2,1)S(1)} %constant_dynamic-update-slice_fusion.9, bf16[2,2,1,32,384]{4,3,2,1,0:T(8,128)(2,1)} %param.11), kind=kLoop, calls=%fused_computation.85 | loop fusion | bytes 196608
  21.1 5.2 %collective-permute-start.4 = (bf16[2,2,4,32,384]{4,3,2,0,1:T(8,128)(2,1)S(1)}, bf16[2,2,4,32,384]{4,3,2,0,1:T(8,128)(2,1)S(1)}, u32[]{:S(2)}, u32[]{:S(2)}) collective-permute-start(bf16[2,2,4,32,384]{4,3,2,0,1:T(8,128)(2,1)S(1)} %copy.70), channel_id=1, source_target_pairs={{0,4},{4,8},{8,12},{1,5},{5,9},{9,13},{2,6},{6,10},{10,14},{3,7},{... | collective-permute-start | bytes 1179656 | tf_op jit(solution)/shard_map/ppermute | solution.py:231
  26.4 1.3 %collective-permute-start.5 = (bf16[2,4,32,384]{3,2,1,0:T(8,128)(2,1)S(1)}, bf16[2,4,32,384]{3,2,1,0:T(8,128)(2,1)S(1)}, u32[]{:S(2)}, u32[]{:S(2)}) collective-permute-start(bf16[2,4,32,384]{3,2,1,0:T(8,128)(2,1)S(1)} %fusion.48), channel_id=1, source_target_pairs={{0,8},{4,12},{1,9},{5,13},{2,10},{6,14},{3,11},{7,15},{16,24},{20,... | collective-permute-start | bytes 589832 | tf_op jit(solution)/shard_map/ppermute | solution.py:232
  27.7 7.5 %collective-permute-done.5 = bf16[2,4,32,384]{3,2,1,0:T(8,128)(2,1)S(1)} collective-permute-done((bf16[2,4,32,384]{3,2,1,0:T(8,128)(2,1)S(1)}, bf16[2,4,32,384]{3,2,1,0:T(8,128)(2,1)S(1)}, u32[]{:S(2)}, u32[]{:S(2)}) %collective-permute-start.5) | collective-permute-done | bytes 196640 | tf_op jit(solution)/shard_map/ppermute | solution.py:232
  35.5 0.5 fusion.45
  36.2 0.2 fusion.51
  36.5 0.4 copy.74
  36.9 0.4 pad.2.clone
  37.4 0.6 fusion.31
  38.0 0.4 copy.73
  38.4 0.4 pad.clone
  38.9 0.6 fusion.30
  39.5 7.0 %convolution_select_fusion = f32[2,4,16,5,384]{4,2,3,1,0:T(8,128)S(1)} fusion(bf16[3,3,3,384,384]{4,3,2,1,0:T(8,128)(2,1)S(1)} %bitcast.55, bf16[2,4,2,8,7,384]{5,2,4,3,1,0:T(2,128)(2,1)S(1)} %fusion.31, pred[16,5]{0,1:T(8,128)(4,1)S(1)} %copy-done.5), kind=kOutput, calls=%fused_computation.5 | convolution fusion | flops 2123612160 | bytes 9633872 | tf_op jit(solution)/shard_map/conv_general_dilated | solution.py:197
  46.6 7.2 %fusion.4 = f32[2,4,16,5,384]{4,2,3,1,0:T(8,128)S(1)} fusion(f32[2,4,16,5,384]{4,2,3,1,0:T(8,128)S(1)} %convolution_select_fusion, bf16[3,3,3,384,384]{4,3,2,1,0:T(8,128)(2,1)S(1)} %bitcast.55, bf16[2,4,2,8,7,384]{5,2,4,3,1,0:T(2,128)(2,1)S(1)} %fusion.30, f32[384]{0:T(512)S(1)} %copy-done.6, pred[16,5]{0,1:T(8,128)(4,1)S(1)} %copy-done.5), kind=kOutput, calls=%fused_computation.8 | convolution fusion | flops 2124103680 | bytes 10618448 | tf_op jit(solution)/shard_map/conv_general_dilated | solution.py:197
  53.8 0.4 copy.66
  54.5 0.4 copy-done.7
  55.1 0.4 copy-done.1
  55.5 0.6 convolution_add_fusion
  56.1 0.2 convolution_add_fusion.2
  56.3 1.0 %convolution_multiply_fusion = f32[4,32,128]{2,1,0:T(8,128)S(1)} fusion(f32[4,32,384]{2,1,0:T(8,128)S(1)} %bitcast.64, f32[4,128,768]{2,1,0:T(8,128)S(1)} %bitcast.56), kind=kOutput, calls=%fused_computation.15 | convolution fusion | flops 75513856 | bytes 1048576 | tf_op jit(solution)/shard_map/nqc,nkc->nqk/dot_general | solution.py:269
  57.4 0.3 convolution_convert_fusion
  58.0 0.7 %fusion.50 = bf16[2,2,1,32,384]{4,3,2,1,0:T(8,128)(2,1)} fusion(bf16[2,2,1,32,384]{4,3,2,1,0:T(8,128)(2,1)S(1)} %bitcast.67, f32[2,2]{1,0:T(2,128)S(1)} %compare_convert_fusion, bf16[2,2,4,32,384]{4,3,2,1,0:T(8,128)(2,1)S(1)} %get-tuple-element.6, s32[]{:T(128)S(6)} %select_n.33), kind=kLoop, calls=%fused_computation.73 | loop fusion | flops 245760 | bytes 294932 | tf_op jit(solution)/shard_map/convert_element_type | solution.py:288
  (56 shorter events, 2.2 us)
Async XLA Ops:
  0.0 57.7 %copy-start = (bf16[384,384]{1,0:T(8,128)(2,1)S(1)}, bf16[384,384]{1,0:T(8,128)(2,1)}, u32[]{:S(2)}) copy-start(bf16[384,384]{1,0:T(8,128)(2,1)} %param.20) | copy-start | bytes 884740
  0.0 20.8 %copy-start.2 = (bf16[2,2,1,32,384]{4,3,2,1,0:T(8,128)(2,1)S(1)}, bf16[2,2,1,32,384]{4,3,2,1,0:T(8,128)(2,1)}, u32[]{:S(2)}) copy-start(bf16[2,2,1,32,384]{4,3,2,1,0:T(8,128)(2,1)} %param.12) | copy-start | bytes 294916
  0.0 20.8 %copy-start.3 = (bf16[2,2,1,32,384]{4,3,2,1,0:T(8,128)(2,1)S(1)}, bf16[2,2,1,32,384]{4,3,2,1,0:T(8,128)(2,1)}, u32[]{:S(2)}) copy-start(bf16[2,2,1,32,384]{4,3,2,1,0:T(8,128)(2,1)} %param.11) | copy-start | bytes 294916
  1.9 10.5 %collective-permute-start = (bf16[4,2,1,32,384]{4,3,2,1,0:T(8,128)(2,1)S(1)}, bf16[4,2,1,32,384]{4,3,2,1,0:T(8,128)(2,1)S(1)}, u32[]{:S(2)}, u32[]{:S(2)}) collective-permute-start(bf16[4,2,1,32,384]{4,3,2,1,0:T(8,128)(2,1)S(1)} %constant_dynamic-update-slice_fusion), channel_id=1, source_target_pairs={{0,1},{1,2},{2,3},{3,0},{4,5},{5,6},{6,7},{7,4},{8,9},{9,10},{10,1... | collective-permute-start | bytes 589832 | tf_op jit(solution)/shard_map/ppermute | solution.py:16
  4.1 16.5 %collective-permute-start.2 = (bf16[4,2,1,32,384]{4,3,2,1,0:T(8,128)(2,1)S(1)}, bf16[4,2,1,32,384]{4,3,2,1,0:T(8,128)(2,1)S(1)}, u32[]{:S(2)}, u32[]{:S(2)}) collective-permute-start(bf16[4,2,1,32,384]{4,3,2,1,0:T(8,128)(2,1)S(1)} %constant_dynamic-update-slice_fusion), channel_id=1, source_target_pairs={{0,3},{1,0},{2,1},{3,2},{4,7},{5,4},{6,5},{7,6},{8,11},{9,8},{10,9... | collective-permute-start | bytes 589832 | tf_op jit(solution)/shard_map/ppermute | solution.py:18
  6.2 6.2 %collective-permute-start.3 = (s32[2]{0:T(128)}, s32[2]{0:T(128)S(1)}, u32[]{:S(2)}, u32[]{:S(2)}) collective-permute-start(s32[2]{0:T(128)} %bitcast.68), channel_id=1, source_target_pairs={{0,4},{4,8},{8,12},{1,5},{5,9},{9,13},{2,6},{6,10},{10,14},{3,7},{... | collective-permute-start | bytes 32 | tf_op jit(solution)/shard_map/ppermute | solution.py:224
  12.4 6.3 %collective-permute-start.1 = (bf16[4,2,1,32,384]{4,3,2,1,0:T(8,128)(2,1)S(1)}, bf16[4,2,1,32,384]{4,3,2,1,0:T(8,128)(2,1)S(1)}, u32[]{:S(2)}, u32[]{:S(2)}) collective-permute-start(bf16[4,2,1,32,384]{4,3,2,1,0:T(8,128)(2,1)S(1)} %collective-permute-done), channel_id=1, source_target_pairs={{0,1},{1,2},{2,3},{3,0},{4,5},{5,6},{6,7},{7,4},{8,9},{9,10},{10,1... | collective-permute-start | bytes 589832 | tf_op jit(solution)/shard_map/ppermute | solution.py:16
  20.7 18.8 %slice-start = ((s8[7962624]{0:T(1024)(128)(4,1)}), s8[4194304]{0:T(1024)(128)(4,1)S(1)}, s32[]{:S(2)}) async-start(s8[7962624]{0:T(1024)(128)(4,1)} %bitcast.54), calls=%async_computation | async-start | bytes 8388608
  20.9 14.7 %copy-start.4 = (f32[384]{0:T(512)S(1)}, f32[384]{0:T(512)}, u32[]{:S(2)}) copy-start(f32[384]{0:T(512)} %param.14) | copy-start | bytes 4612
  21.1 14.2 %collective-permute-start.4 = (bf16[2,2,4,32,384]{4,3,2,0,1:T(8,128)(2,1)S(1)}, bf16[2,2,4,32,384]{4,3,2,0,1:T(8,128)(2,1)S(1)}, u32[]{:S(2)}, u32[]{:S(2)}) collective-permute-start(bf16[2,2,4,32,384]{4,3,2,0,1:T(8,128)(2,1)S(1)} %copy.70), channel_id=1, source_target_pairs={{0,4},{4,8},{8,12},{1,5},{5,9},{9,13},{2,6},{6,10},{10,14},{3,7},{... | collective-permute-start | bytes 1179656 | tf_op jit(solution)/shard_map/ppermute | solution.py:231
  26.4 8.8 %collective-permute-start.5 = (bf16[2,4,32,384]{3,2,1,0:T(8,128)(2,1)S(1)}, bf16[2,4,32,384]{3,2,1,0:T(8,128)(2,1)S(1)}, u32[]{:S(2)}, u32[]{:S(2)}) collective-permute-start(bf16[2,4,32,384]{3,2,1,0:T(8,128)(2,1)S(1)} %fusion.48), channel_id=1, source_target_pairs={{0,8},{4,12},{1,9},{5,13},{2,10},{6,14},{3,11},{7,15},{16,24},{20,... | collective-permute-start | bytes 589832 | tf_op jit(solution)/shard_map/ppermute | solution.py:232
  36.2 3.3 %slice-start.1 = ((s8[7962624]{0:T(1024)(128)(4,1)}), s8[3768320]{0:T(1024)(128)(4,1)S(1)}, s32[]{:S(2)}) async-start(s8[7962624]{0:T(1024)(128)(4,1)} %bitcast.54), calls=%async_computation.1 | async-start | bytes 7536640
  38.0 1.5 %copy-start.5 = (pred[16,5]{0,1:T(8,128)(4,1)S(1)}, pred[16,5]{0,1:T(8,128)(4,1)}, u32[]{:S(2)}) copy-start(pred[16,5]{0,1:T(8,128)(4,1)} %constant.67) | copy-start | bytes 244
  39.5 7.0 %copy-start.6 = (f32[384]{0:T(512)S(1)}, f32[384]{0:T(512)}, u32[]{:S(2)}) copy-start(f32[384]{0:T(512)} %param.16) | copy-start | bytes 4612
  54.2 0.7 %copy-start.7 = (f32[384]{0:T(512)S(1)}, f32[384]{0:T(512)}, u32[]{:S(2)}) copy-start(f32[384]{0:T(512)} %param.17) | copy-start | bytes 4612
  54.3 1.2 %copy-start.1 = (bf16[384,1152]{1,0:T(8,128)(2,1)S(1)}, bf16[384,1152]{1,0:T(8,128)(2,1)}, u32[]{:S(2)}) copy-start(bf16[384,1152]{1,0:T(8,128)(2,1)} %param.18) | copy-start | bytes 2654212
  55.1 1.0 %slice-start.2 = ((f32[1152]{0:T(1024)}), f32[384]{0:T(512)S(1)}, s32[]{:S(2)}) async-start(f32[1152]{0:T(1024)} %param.19), calls=%async_computation.2 | async-start | bytes 4096 | tf_op jit(solution)/shard_map/slice | solution.py:267
  56.0 1.7 %copy-start.8 = (f32[384]{0:T(512)S(1)}, f32[384]{0:T(512)}, u32[]{:S(2)}) copy-start(f32[384]{0:T(512)} %param.21) | copy-start | bytes 4612
